TPU v7x, 512 devices: a whole 4x4x16 slice. The times are simulated.
512 devices in a mesh: row: 16 (over z), col: 4 (over x_hi, core), depth: 8 (over y, x_lo).
Axes of the slice: x: 4 (x_hi: 2, x_lo: 2; x = x_hi * 2 + x_lo), y: 4, z: 16, core: 2. Of those that a mesh axis runs over, the one named last changes fastest.
Arguments:
- ks_matrix: bfloat16 [4096, 16384], P('col', ('row', 'depth')), may hold values from -6 to 6
- sign_matrix: bfloat16 [16, 8, 128, 12288], P('col', 'depth', None, 'row'), may hold values from -0.046875 to 0.046875
- ks_mask: int32 [32, 128], P('col', ('row', 'depth')), may hold values 0 or 1
- sign_mask: int32 [16, 8, 1, 96], P('col', 'depth', None, 'row'), may hold values 0 or 1
- product_mask: int32 [32, 96], P('col', 'row'), may hold values 0 or 1
- row_order: int32 [4, 8], P('col'), may hold values from 0 to 7, each once within a row
Outputs:
- next_matrix: bfloat16 [4096, 12288], P(('col', 'depth'), 'row')
Inputs may be any that keep to these rules, and one draw needn't show every extreme that they name: Each row of row_order names every number of 0 to 7 once.
All inputs are finite; a program needn't handle non-finite values. No bound on the sum of `ks_mask` or of `sign_mask` or of `product_mask` on one device may be relied on, other than what follows from the above.
Results may differ from a plain program's by a relative error of at most 0.001.
Values may be sent and summed in bfloat16 or wider, within the bound.
No kernel may reach another device: no remote copies, remote signals or barrier semaphores. Data moves between devices by JAX's collectives and lax.ppermute only.
A program may use at most 64 MiB of HBM per device.

v0:
```python
import jax
import jax.numpy as jnp
from jax import lax
from jax.sharding import PartitionSpec as P

BS = 128


def from_behind(block, axis, distance):
    devices = range(lax.axis_size(axis))
    route = [((i - distance) % len(devices), i) for i in devices]
    return lax.ppermute(block, axis, route)


def per_device(ks_matrix, sign_matrix, ks_mask, sign_mask, product_mask, row_order):
    row_blocks, inner_blocks = ks_mask.shape
    local_groups = sign_mask.shape[0]
    sign_inner = sign_mask.shape[2]
    col_blocks = sign_mask.shape[3]
    ks_panel = (
        ks_matrix.reshape(row_blocks, BS, inner_blocks, BS)
        * ks_mask.astype(jnp.bfloat16)[:, None, :, None]
    )
    ks_panel = ks_panel.reshape(row_blocks * BS, inner_blocks * BS)
    sign_kept = sign_matrix.reshape(local_groups, sign_inner, BS, col_blocks, BS)
    sign_kept = sign_kept * sign_mask.astype(jnp.bfloat16).reshape(
        local_groups, sign_inner, 1, col_blocks, 1
    )
    sign_kept = sign_kept.reshape(local_groups, 1, sign_inner * BS, col_blocks * BS)
    sign_whole = lax.all_gather(sign_kept, "col", axis=0, tiled=True)
    row_count = lax.axis_size("row")
    start_sum = jnp.zeros((row_blocks * BS, col_blocks * BS), jnp.float32)
    row_index = lax.axis_index("row")

    def advance(step, carry):
        running, moving = carry
        source = (row_index - step) % row_count
        sign_piece = lax.dynamic_index_in_dim(sign_whole, source, 0, keepdims=False)[0]
        running = running + jnp.dot(moving, sign_piece, preferred_element_type=jnp.float32)
        moving = from_behind(moving, "row", 1)
        return (running, moving)

    running, moving = lax.fori_loop(0, row_count - 1, advance, (start_sum, ks_panel))
    final_source = (row_index - row_count + 1) % row_count
    final_piece = lax.dynamic_index_in_dim(sign_whole, final_source, 0, keepdims=False)[0]
    running = running + jnp.dot(moving, final_piece, preferred_element_type=jnp.float32)
    depth_count = lax.axis_size("depth")
    part_rows = row_blocks // depth_count
    filtered = (
        running.reshape(row_blocks, BS, col_blocks, BS)
        * product_mask.astype(jnp.float32)[:, None, :, None]
    )
    local_order = row_order[0]
    summed = lax.psum(filtered, "depth")
    own_rows = lax.dynamic_slice_in_dim(
        local_order, lax.axis_index("depth") * part_rows, part_rows, 0
    )
    picked = jnp.take(summed, own_rows, axis=0)
    return picked.reshape(part_rows * BS, col_blocks * BS).astype(jnp.bfloat16)


def solution(mesh):
    in_specs = (
        P("col", ("row", "depth")),
        P("col", "depth", None, "row"),
        P("col", ("row", "depth")),
        P("col", "depth", None, "row"),
        P("col", "row"),
        P("col", None),
    )
    out_specs = P(("col", "depth"), "row")
    return jax.shard_map(
        per_device, mesh=mesh, in_specs=in_specs, out_specs=out_specs, check_vma=False
    )
```

profile of v0, /device:TPU:4, one launch (start us, length us, event | category | flops | bytes accessed | tf_op | source)
XLA Modules:
  0.0 356.8 jit_solution(18374426383536028386)
XLA Ops:
  7.3 2.1 broadcast_multiply_fusion.1
  15.4 36.3 %all-gather.2.cloned.1.call-done = bf16[16,1,128,768]{3,2,1,0:T(8,128)(2,1)} async-done(((bf16[4,1,128,768]{3,2,1,0:T(8,128)(2,1)}), bf16[16,1,128,768]{3,2,1,0:T(8,128)(2,1)}) %all-gather.2.cloned.1.call-update) | async-done | bytes 3145744 | tf_op jit(solution)/shard_map/all_gather | solution.py:30
  51.6 171.1 %while.19 = (s32[]{:T(128)}, f32[1024,768]{0,1:T(8,128)S(1)}, bf16[1024,128]{1,0:T(8,128)(2,1)}, s32[]{:T(128)}, bf16[16,1,128,768]{3,2,1,0:T(8,128)(2,1)}, /*index=5*/s32[]{:T(128)}, s32[]{:T(128)}, s32[]{:T(128)}, s32[]{:T(128)}) while((s32[]{:T(128)}, f32[1024,768]{0,1:T(8,128)S(1)}, bf16[1024,128]{1,0:T(8,128)(2,1)}, ...), condition=%wide.region_1.2_spmd.clone, body=%wide.region_0.1_spmd.clone.sunk | while | flops 202899472 | bytes 8323374 | solution.py:43
  52.6 3.7 %collective-permute-start = (bf16[1024,128]{1,0:T(8,128)(2,1)S(1)}, bf16[1024,128]{1,0:T(8,128)(2,1)}, u32[]{:S(2)}, u32[]{:S(2)}) collective-permute-start(bf16[1024,128]{1,0:T(8,128)(2,1)S(1)} %copy.29), channel_id=1, source_target_pairs={{480,0},{0,32},{32,64},{64,96},{96,128},{128,160},{160,192},{192,2... | collective-permute-start | bytes 786440 | tf_op jit(solution)/shard_map/while/body/eval_jaxpr/ppermute | solution.py:12
  58.2 7.4 %collective-permute-done = bf16[1024,128]{1,0:T(8,128)(2,1)} collective-permute-done((bf16[1024,128]{1,0:T(8,128)(2,1)S(1)}, bf16[1024,128]{1,0:T(8,128)(2,1)}, u32[]{:S(2)}, u32[]{:S(2)}) %collective-permute-start) | collective-permute-done | bytes 262176 | tf_op jit(solution)/shard_map/while/body/eval_jaxpr/ppermute | solution.py:12
  70.3 7.3 %collective-permute-done = bf16[1024,128]{1,0:T(8,128)(2,1)} collective-permute-done((bf16[1024,128]{1,0:T(8,128)(2,1)S(1)}, bf16[1024,128]{1,0:T(8,128)(2,1)}, u32[]{:S(2)}, u32[]{:S(2)}) %collective-permute-start) | collective-permute-done | bytes 262176 | tf_op jit(solution)/shard_map/while/body/eval_jaxpr/ppermute | solution.py:12
  82.4 6.5 %collective-permute-done = bf16[1024,128]{1,0:T(8,128)(2,1)} collective-permute-done((bf16[1024,128]{1,0:T(8,128)(2,1)S(1)}, bf16[1024,128]{1,0:T(8,128)(2,1)}, u32[]{:S(2)}, u32[]{:S(2)}) %collective-permute-start) | collective-permute-done | bytes 262176 | tf_op jit(solution)/shard_map/while/body/eval_jaxpr/ppermute | solution.py:12
  93.7 5.7 %collective-permute-done = bf16[1024,128]{1,0:T(8,128)(2,1)} collective-permute-done((bf16[1024,128]{1,0:T(8,128)(2,1)S(1)}, bf16[1024,128]{1,0:T(8,128)(2,1)}, u32[]{:S(2)}, u32[]{:S(2)}) %collective-permute-start) | collective-permute-done | bytes 262176 | tf_op jit(solution)/shard_map/while/body/eval_jaxpr/ppermute | solution.py:12
  104.2 5.7 %collective-permute-done = bf16[1024,128]{1,0:T(8,128)(2,1)} collective-permute-done((bf16[1024,128]{1,0:T(8,128)(2,1)S(1)}, bf16[1024,128]{1,0:T(8,128)(2,1)}, u32[]{:S(2)}, u32[]{:S(2)}) %collective-permute-start) | collective-permute-done | bytes 262176 | tf_op jit(solution)/shard_map/while/body/eval_jaxpr/ppermute | solution.py:12
  114.7 5.7 %collective-permute-done = bf16[1024,128]{1,0:T(8,128)(2,1)} collective-permute-done((bf16[1024,128]{1,0:T(8,128)(2,1)S(1)}, bf16[1024,128]{1,0:T(8,128)(2,1)}, u32[]{:S(2)}, u32[]{:S(2)}) %collective-permute-start) | collective-permute-done | bytes 262176 | tf_op jit(solution)/shard_map/while/body/eval_jaxpr/ppermute | solution.py:12
  125.2 5.7 %collective-permute-done = bf16[1024,128]{1,0:T(8,128)(2,1)} collective-permute-done((bf16[1024,128]{1,0:T(8,128)(2,1)S(1)}, bf16[1024,128]{1,0:T(8,128)(2,1)}, u32[]{:S(2)}, u32[]{:S(2)}) %collective-permute-start) | collective-permute-done | bytes 262176 | tf_op jit(solution)/shard_map/while/body/eval_jaxpr/ppermute | solution.py:12
  135.8 6.7 %collective-permute-done = bf16[1024,128]{1,0:T(8,128)(2,1)} collective-permute-done((bf16[1024,128]{1,0:T(8,128)(2,1)S(1)}, bf16[1024,128]{1,0:T(8,128)(2,1)}, u32[]{:S(2)}, u32[]{:S(2)}) %collective-permute-start) | collective-permute-done | bytes 262176 | tf_op jit(solution)/shard_map/while/body/eval_jaxpr/ppermute | solution.py:12
  147.3 7.9 %collective-permute-done = bf16[1024,128]{1,0:T(8,128)(2,1)} collective-permute-done((bf16[1024,128]{1,0:T(8,128)(2,1)S(1)}, bf16[1024,128]{1,0:T(8,128)(2,1)}, u32[]{:S(2)}, u32[]{:S(2)}) %collective-permute-start) | collective-permute-done | bytes 262176 | tf_op jit(solution)/shard_map/while/body/eval_jaxpr/ppermute | solution.py:12
  160.0 8.0 %collective-permute-done = bf16[1024,128]{1,0:T(8,128)(2,1)} collective-permute-done((bf16[1024,128]{1,0:T(8,128)(2,1)S(1)}, bf16[1024,128]{1,0:T(8,128)(2,1)}, u32[]{:S(2)}, u32[]{:S(2)}) %collective-permute-start) | collective-permute-done | bytes 262176 | tf_op jit(solution)/shard_map/while/body/eval_jaxpr/ppermute | solution.py:12
  172.8 7.2 %collective-permute-done = bf16[1024,128]{1,0:T(8,128)(2,1)} collective-permute-done((bf16[1024,128]{1,0:T(8,128)(2,1)S(1)}, bf16[1024,128]{1,0:T(8,128)(2,1)}, u32[]{:S(2)}, u32[]{:S(2)}) %collective-permute-start) | collective-permute-done | bytes 262176 | tf_op jit(solution)/shard_map/while/body/eval_jaxpr/ppermute | solution.py:12
  184.8 6.3 %collective-permute-done = bf16[1024,128]{1,0:T(8,128)(2,1)} collective-permute-done((bf16[1024,128]{1,0:T(8,128)(2,1)S(1)}, bf16[1024,128]{1,0:T(8,128)(2,1)}, u32[]{:S(2)}, u32[]{:S(2)}) %collective-permute-start) | collective-permute-done | bytes 262176 | tf_op jit(solution)/shard_map/while/body/eval_jaxpr/ppermute | solution.py:12
  195.9 5.7 %collective-permute-done = bf16[1024,128]{1,0:T(8,128)(2,1)} collective-permute-done((bf16[1024,128]{1,0:T(8,128)(2,1)S(1)}, bf16[1024,128]{1,0:T(8,128)(2,1)}, u32[]{:S(2)}, u32[]{:S(2)}) %collective-permute-start) | collective-permute-done | bytes 262176 | tf_op jit(solution)/shard_map/while/body/eval_jaxpr/ppermute | solution.py:12
  206.4 5.7 %collective-permute-done = bf16[1024,128]{1,0:T(8,128)(2,1)} collective-permute-done((bf16[1024,128]{1,0:T(8,128)(2,1)S(1)}, bf16[1024,128]{1,0:T(8,128)(2,1)}, u32[]{:S(2)}, u32[]{:S(2)}) %collective-permute-start) | collective-permute-done | bytes 262176 | tf_op jit(solution)/shard_map/while/body/eval_jaxpr/ppermute | solution.py:12
  217.0 5.7 %collective-permute-done = bf16[1024,128]{1,0:T(8,128)(2,1)} collective-permute-done((bf16[1024,128]{1,0:T(8,128)(2,1)S(1)}, bf16[1024,128]{1,0:T(8,128)(2,1)}, u32[]{:S(2)}, u32[]{:S(2)}) %collective-permute-start) | collective-permute-done | bytes 262176 | tf_op jit(solution)/shard_map/while/body/eval_jaxpr/ppermute | solution.py:12
  222.7 2.4 copy.12
  225.1 2.6 convolution_add_fusion
  227.7 2.3 copy.13
  230.0 2.6 copy.19
  233.0 114.2 %all-reduce.1 = bf16[8,128,6,128]{1,0,3,2:T(8,128)(2,1)} all-reduce(f32[8,128,6,128]{1,0,3,2:T(8,128)S(1)} %broadcast_multiply_fusion), channel_id=1, replica_groups=mesh['row'=16,'col'=4,'depth'=8] {'depth'}, use_global_device_ids=true, to_apply=%region_2.3 | all-reduce | flops 786432 | bytes 4718592 | tf_op jit(solution)/shard_map/psum | solution.py:54
  (63 shorter events, 76.9 us)
Async XLA Ops:
  6.5 3.7 %copy-start = (s32[1,8]{1,0:T(1,128)S(1)}, s32[1,8]{1,0:T(1,128)}, u32[]{:S(2)}) copy-start(s32[1,8]{1,0:T(1,128)} %param.13) | copy-start | bytes 100
  6.5 45.1 %all-gather.2.cloned.1.call-start = ((), (), s32[]{:S(2)}) async-start(), calls=%async_computation | async-start | bytes 3932160 | tf_op jit(solution)/shard_map/all_gather | solution.py:30
  52.6 13.0 %collective-permute-start = (bf16[1024,128]{1,0:T(8,128)(2,1)S(1)}, bf16[1024,128]{1,0:T(8,128)(2,1)}, u32[]{:S(2)}, u32[]{:S(2)}) collective-permute-start(bf16[1024,128]{1,0:T(8,128)(2,1)S(1)} %copy.29), channel_id=1, source_target_pairs={{480,0},{0,32},{32,64},{64,96},{96,128},{128,160},{160,192},{192,2... | collective-permute-start | bytes 786440 | tf_op jit(solution)/shard_map/while/body/eval_jaxpr/ppermute | solution.py:12
  66.5 11.2 %collective-permute-start = (bf16[1024,128]{1,0:T(8,128)(2,1)S(1)}, bf16[1024,128]{1,0:T(8,128)(2,1)}, u32[]{:S(2)}, u32[]{:S(2)}) collective-permute-start(bf16[1024,128]{1,0:T(8,128)(2,1)S(1)} %copy.29), channel_id=1, source_target_pairs={{480,0},{0,32},{32,64},{64,96},{96,128},{128,160},{160,192},{192,2... | collective-permute-start | bytes 786440 | tf_op jit(solution)/shard_map/while/body/eval_jaxpr/ppermute | solution.py:12
  78.6 10.3 %collective-permute-start = (bf16[1024,128]{1,0:T(8,128)(2,1)S(1)}, bf16[1024,128]{1,0:T(8,128)(2,1)}, u32[]{:S(2)}, u32[]{:S(2)}) collective-permute-start(bf16[1024,128]{1,0:T(8,128)(2,1)S(1)} %copy.29), channel_id=1, source_target_pairs={{480,0},{0,32},{32,64},{64,96},{96,128},{128,160},{160,192},{192,2... | collective-permute-start | bytes 786440 | tf_op jit(solution)/shard_map/while/body/eval_jaxpr/ppermute | solution.py:12
  89.9 9.6 %collective-permute-start = (bf16[1024,128]{1,0:T(8,128)(2,1)S(1)}, bf16[1024,128]{1,0:T(8,128)(2,1)}, u32[]{:S(2)}, u32[]{:S(2)}) collective-permute-start(bf16[1024,128]{1,0:T(8,128)(2,1)S(1)} %copy.29), channel_id=1, source_target_pairs={{480,0},{0,32},{32,64},{64,96},{96,128},{128,160},{160,192},{192,2... | collective-permute-start | bytes 786440 | tf_op jit(solution)/shard_map/while/body/eval_jaxpr/ppermute | solution.py:12
  100.4 9.6 %collective-permute-start = (bf16[1024,128]{1,0:T(8,128)(2,1)S(1)}, bf16[1024,128]{1,0:T(8,128)(2,1)}, u32[]{:S(2)}, u32[]{:S(2)}) collective-permute-start(bf16[1024,128]{1,0:T(8,128)(2,1)S(1)} %copy.29), channel_id=1, source_target_pairs={{480,0},{0,32},{32,64},{64,96},{96,128},{128,160},{160,192},{192,2... | collective-permute-start | bytes 786440 | tf_op jit(solution)/shard_map/while/body/eval_jaxpr/ppermute | solution.py:12
  110.9 9.6 %collective-permute-start = (bf16[1024,128]{1,0:T(8,128)(2,1)S(1)}, bf16[1024,128]{1,0:T(8,128)(2,1)}, u32[]{:S(2)}, u32[]{:S(2)}) collective-permute-start(bf16[1024,128]{1,0:T(8,128)(2,1)S(1)} %copy.29), channel_id=1, source_target_pairs={{480,0},{0,32},{32,64},{64,96},{96,128},{128,160},{160,192},{192,2... | collective-permute-start | bytes 786440 | tf_op jit(solution)/shard_map/while/body/eval_jaxpr/ppermute | solution.py:12
  121.4 9.6 %collective-permute-start = (bf16[1024,128]{1,0:T(8,128)(2,1)S(1)}, bf16[1024,128]{1,0:T(8,128)(2,1)}, u32[]{:S(2)}, u32[]{:S(2)}) collective-permute-start(bf16[1024,128]{1,0:T(8,128)(2,1)S(1)} %copy.29), channel_id=1, source_target_pairs={{480,0},{0,32},{32,64},{64,96},{96,128},{128,160},{160,192},{192,2... | collective-permute-start | bytes 786440 | tf_op jit(solution)/shard_map/while/body/eval_jaxpr/ppermute | solution.py:12
  131.9 10.6 %collective-permute-start = (bf16[1024,128]{1,0:T(8,128)(2,1)S(1)}, bf16[1024,128]{1,0:T(8,128)(2,1)}, u32[]{:S(2)}, u32[]{:S(2)}) collective-permute-start(bf16[1024,128]{1,0:T(8,128)(2,1)S(1)} %copy.29), channel_id=1, source_target_pairs={{480,0},{0,32},{32,64},{64,96},{96,128},{128,160},{160,192},{192,2... | collective-permute-start | bytes 786440 | tf_op jit(solution)/shard_map/while/body/eval_jaxpr/ppermute | solution.py:12
  143.5 11.8 %collective-permute-start = (bf16[1024,128]{1,0:T(8,128)(2,1)S(1)}, bf16[1024,128]{1,0:T(8,128)(2,1)}, u32[]{:S(2)}, u32[]{:S(2)}) collective-permute-start(bf16[1024,128]{1,0:T(8,128)(2,1)S(1)} %copy.29), channel_id=1, source_target_pairs={{480,0},{0,32},{32,64},{64,96},{96,128},{128,160},{160,192},{192,2... | collective-permute-start | bytes 786440 | tf_op jit(solution)/shard_map/while/body/eval_jaxpr/ppermute | solution.py:12
  156.2 11.8 %collective-permute-start = (bf16[1024,128]{1,0:T(8,128)(2,1)S(1)}, bf16[1024,128]{1,0:T(8,128)(2,1)}, u32[]{:S(2)}, u32[]{:S(2)}) collective-permute-start(bf16[1024,128]{1,0:T(8,128)(2,1)S(1)} %copy.29), channel_id=1, source_target_pairs={{480,0},{0,32},{32,64},{64,96},{96,128},{128,160},{160,192},{192,2... | collective-permute-start | bytes 786440 | tf_op jit(solution)/shard_map/while/body/eval_jaxpr/ppermute | solution.py:12
  169.0 11.1 %collective-permute-start = (bf16[1024,128]{1,0:T(8,128)(2,1)S(1)}, bf16[1024,128]{1,0:T(8,128)(2,1)}, u32[]{:S(2)}, u32[]{:S(2)}) collective-permute-start(bf16[1024,128]{1,0:T(8,128)(2,1)S(1)} %copy.29), channel_id=1, source_target_pairs={{480,0},{0,32},{32,64},{64,96},{96,128},{128,160},{160,192},{192,2... | collective-permute-start | bytes 786440 | tf_op jit(solution)/shard_map/while/body/eval_jaxpr/ppermute | solution.py:12
  181.0 10.2 %collective-permute-start = (bf16[1024,128]{1,0:T(8,128)(2,1)S(1)}, bf16[1024,128]{1,0:T(8,128)(2,1)}, u32[]{:S(2)}, u32[]{:S(2)}) collective-permute-start(bf16[1024,128]{1,0:T(8,128)(2,1)S(1)} %copy.29), channel_id=1, source_target_pairs={{480,0},{0,32},{32,64},{64,96},{96,128},{128,160},{160,192},{192,2... | collective-permute-start | bytes 786440 | tf_op jit(solution)/shard_map/while/body/eval_jaxpr/ppermute | solution.py:12
  192.1 9.6 %collective-permute-start = (bf16[1024,128]{1,0:T(8,128)(2,1)S(1)}, bf16[1024,128]{1,0:T(8,128)(2,1)}, u32[]{:S(2)}, u32[]{:S(2)}) collective-permute-start(bf16[1024,128]{1,0:T(8,128)(2,1)S(1)} %copy.29), channel_id=1, source_target_pairs={{480,0},{0,32},{32,64},{64,96},{96,128},{128,160},{160,192},{192,2... | collective-permute-start | bytes 786440 | tf_op jit(solution)/shard_map/while/body/eval_jaxpr/ppermute | solution.py:12
  202.6 9.6 %collective-permute-start = (bf16[1024,128]{1,0:T(8,128)(2,1)S(1)}, bf16[1024,128]{1,0:T(8,128)(2,1)}, u32[]{:S(2)}, u32[]{:S(2)}) collective-permute-start(bf16[1024,128]{1,0:T(8,128)(2,1)S(1)} %copy.29), channel_id=1, source_target_pairs={{480,0},{0,32},{32,64},{64,96},{96,128},{128,160},{160,192},{192,2... | collective-permute-start | bytes 786440 | tf_op jit(solution)/shard_map/while/body/eval_jaxpr/ppermute | solution.py:12
  213.1 9.6 %collective-permute-start = (bf16[1024,128]{1,0:T(8,128)(2,1)S(1)}, bf16[1024,128]{1,0:T(8,128)(2,1)}, u32[]{:S(2)}, u32[]{:S(2)}) collective-permute-start(bf16[1024,128]{1,0:T(8,128)(2,1)S(1)} %copy.29), channel_id=1, source_target_pairs={{480,0},{0,32},{32,64},{64,96},{96,128},{128,160},{160,192},{192,2... | collective-permute-start | bytes 786440 | tf_op jit(solution)/shard_map/while/body/eval_jaxpr/ppermute | solution.py:12
Sparse Core Ops, SparseCore 0:
  9.5 42.0 all-gather.1
where the time goes:
time: 358 us; the launch traced here: 357 us
  waiting for transfers between devices  134 us (37%)
  blocking collectives  114 us (32%)
  matrix products  30.7 us (9%)
  starting transfers between devices  30.4 us (8%)
  local copies, waits for them, and re-layouts  23.3 us (7%)
  between operations  15.4 us (4%)
  other arithmetic  8.19 us (2%)
    psum x1, blocking collectives, per_device(): summed = lax.psum(filtered, 'depth')  114 us
    ppermute x15, waiting for transfers between devices, from_behind(): return lax.ppermute(block, axis, route)  97.7 us
    all_gather x1, waiting for transfers between devices, per_device(): sign_whole = lax.all_gather(sign_kept, 'col', axis=0, tiled=True)  36.3 us
    ppermute x15, starting transfers between devices, from_behind(): return lax.ppermute(block, axis, route)  30.4 us
    dot_general x15, matrix products, advance(): jnp.dot(moving, sign_piece, preferred_element_type=jnp.float32)  28.1 us
    while x15, local copies, waits for them, and re-layouts  14.3 us
  transfers between devices with their start and end apart: 16, of which 16 were waited for; matrix products, arithmetic and copies ran while one was open for 9% of the time, Pallas kernels for 0%

commit v1 on v0

--- a/solution.py
+++ b/solution.py
@@ -1,9 +1,25 @@
+import functools
 import jax
 import jax.numpy as jnp
 from jax import lax
 from jax.sharding import PartitionSpec as P
 
 BS = 128
+
+
+def match_shelves(xx, along_dim):
+    return jnp.concatenate(
+        lax.all_to_all(
+            jnp.stack([xx] * lax.psum(1, axis_name="col")),
+            axis_name="col",
+            split_axis=0,
+            concat_axis=0,
+        ),
+        axis=along_dim,
+    )
+
+
+search_rounds_by_axis = functools.partial(match_shelves, along_dim=0)
 
 
 def from_behind(block, axis, distance):
@@ -27,7 +43,7 @@
         local_groups, sign_inner, 1, col_blocks, 1
     )
     sign_kept = sign_kept.reshape(local_groups, 1, sign_inner * BS, col_blocks * BS)
-    sign_whole = lax.all_gather(sign_kept, "col", axis=0, tiled=True)
+    sign_whole = search_rounds_by_axis(sign_kept)
     row_count = lax.axis_size("row")
     start_sum = jnp.zeros((row_blocks * BS, col_blocks * BS), jnp.float32)
     row_index = lax.axis_index("row")

time: 358 us -> 349 us (0.975)
  between operations: 15.4 us -> 2.02 us
  starting transfers between devices: 30.4 us -> 39.3 us
  waiting for transfers between devices: 134 us -> 130 us
    all_gather x1 -> x0, waiting for transfers between devices: 36.3 us -> none  [per_device(): sign_whole = lax.all_gather(sign_kept, 'col', axis=0, tiled=True)]
    all_to_all x0 -> x1, waiting for transfers between devices: none -> 31.8 us  [match_shelves(): lax.all_to_all(jnp.stack([xx] * lax.psum(1, axis_name='col')), axis_name=...]
    all_to_all x0 -> x1, starting transfers between devices: none -> 10.6 us  [match_shelves(): lax.all_to_all(jnp.stack([xx] * lax.psum(1, axis_name='col')), axis_name=...]
where the time goes in v1:
time: 349 us; the launch traced here: 347 us
  waiting for transfers between devices  130 us (37%)
  blocking collectives  114 us (33%)
  starting transfers between devices  39.3 us (11%)
  matrix products  30.7 us (9%)
  local copies, waits for them, and re-layouts  25.3 us (7%)
  other arithmetic  5.23 us (1%)
    psum x1, blocking collectives, per_device(): summed = lax.psum(filtered, 'depth')  114 us
    ppermute x15, waiting for transfers between devices, from_behind(): return lax.ppermute(block, axis, route)  98 us
    all_to_all x1, waiting for transfers between devices, match_shelves(): lax.all_to_all(jnp.stack([xx] * lax.psum(1, axis_name='col')), axis_name=...  31.8 us
    ppermute x15, starting transfers between devices, from_behind(): return lax.ppermute(block, axis, route)  28.6 us
    dot_general x15, matrix products, advance(): jnp.dot(moving, sign_piece, preferred_element_type=jnp.float32)  28.1 us
    while x15, local copies, waits for them, and re-layouts  14.3 us
    all_to_all x1, starting transfers between devices, match_shelves(): lax.all_to_all(jnp.stack([xx] * lax.psum(1, axis_name='col')), axis_name=...  10.6 us
  transfers between devices with their start and end apart: 16, of which 16 were waited for; matrix products, arithmetic and copies ran while one was open for 9% of the time, Pallas kernels for 0%

profile of v1, /device:TPU:4, one launch (start us, length us, event | category | flops | bytes accessed | tf_op | source)
XLA Modules:
  0.0 347.3 jit_solution(16675154711232431685)
XLA Ops:
  2.0 2.0 stack.3
  4.0 10.6 %all-to-all-start = ((bf16[4,4,1,128,768]{4,3,1,2,0:T(8,128)(2,1)}), bf16[4,4,1,128,768]{4,3,1,2,0:T(8,128)(2,1)}, u32[]{:S(2)}, u32[]{:S(2)}) async-start(bf16[4,4,1,128,768]{4,3,1,2,0:T(8,128)(2,1)} %stack.3), calls=%async_computation | async-start | bytes 6291456 | tf_op jit(solution)/shard_map/all_to_all | solution.py:12
  18.2 31.8 %all-to-all-done = bf16[4,4,1,128,768]{4,3,1,2,0:T(8,128)(2,1)} async-done(((bf16[4,4,1,128,768]{4,3,1,2,0:T(8,128)(2,1)}), bf16[4,4,1,128,768]{4,3,1,2,0:T(8,128)(2,1)}, u32[]{:S(2)}, u32[]{:S(2)}) %all-to-all-start) | async-done | bytes 3145760 | tf_op jit(solution)/shard_map/all_to_all | solution.py:12
  50.0 169.7 %while.19 = (s32[]{:T(128)}, f32[1024,768]{0,1:T(8,128)S(1)}, bf16[1024,128]{1,0:T(8,128)(2,1)}, s32[]{:T(128)}, bf16[16,1,128,768]{3,2,1,0:T(8,128)(2,1)}, /*index=5*/s32[]{:T(128)}, s32[]{:T(128)}, s32[]{:T(128)}, s32[]{:T(128)}) while((s32[]{:T(128)}, f32[1024,768]{0,1:T(8,128)S(1)}, bf16[1024,128]{1,0:T(8,128)(2,1)}, ...), condition=%wide.region_1.2_spmd.clone, body=%wide.region_0.1_spmd.clone.sunk | while | flops 202899472 | bytes 8323374 | solution.py:59
  54.8 8.7 %collective-permute-done = bf16[1024,128]{1,0:T(8,128)(2,1)} collective-permute-done((bf16[1024,128]{1,0:T(8,128)(2,1)S(1)}, bf16[1024,128]{1,0:T(8,128)(2,1)}, u32[]{:S(2)}, u32[]{:S(2)}) %collective-permute-start) | collective-permute-done | bytes 262176 | tf_op jit(solution)/shard_map/while/body/eval_jaxpr/ppermute | solution.py:28
  68.2 6.9 %collective-permute-done = bf16[1024,128]{1,0:T(8,128)(2,1)} collective-permute-done((bf16[1024,128]{1,0:T(8,128)(2,1)S(1)}, bf16[1024,128]{1,0:T(8,128)(2,1)}, u32[]{:S(2)}, u32[]{:S(2)}) %collective-permute-start) | collective-permute-done | bytes 262176 | tf_op jit(solution)/shard_map/while/body/eval_jaxpr/ppermute | solution.py:28
  79.9 6.0 %collective-permute-done = bf16[1024,128]{1,0:T(8,128)(2,1)} collective-permute-done((bf16[1024,128]{1,0:T(8,128)(2,1)S(1)}, bf16[1024,128]{1,0:T(8,128)(2,1)}, u32[]{:S(2)}, u32[]{:S(2)}) %collective-permute-start) | collective-permute-done | bytes 262176 | tf_op jit(solution)/shard_map/while/body/eval_jaxpr/ppermute | solution.py:28
  90.7 5.7 %collective-permute-done = bf16[1024,128]{1,0:T(8,128)(2,1)} collective-permute-done((bf16[1024,128]{1,0:T(8,128)(2,1)S(1)}, bf16[1024,128]{1,0:T(8,128)(2,1)}, u32[]{:S(2)}, u32[]{:S(2)}) %collective-permute-start) | collective-permute-done | bytes 262176 | tf_op jit(solution)/shard_map/while/body/eval_jaxpr/ppermute | solution.py:28
  101.2 5.7 %collective-permute-done = bf16[1024,128]{1,0:T(8,128)(2,1)} collective-permute-done((bf16[1024,128]{1,0:T(8,128)(2,1)S(1)}, bf16[1024,128]{1,0:T(8,128)(2,1)}, u32[]{:S(2)}, u32[]{:S(2)}) %collective-permute-start) | collective-permute-done | bytes 262176 | tf_op jit(solution)/shard_map/while/body/eval_jaxpr/ppermute | solution.py:28
  111.8 5.7 %collective-permute-done = bf16[1024,128]{1,0:T(8,128)(2,1)} collective-permute-done((bf16[1024,128]{1,0:T(8,128)(2,1)S(1)}, bf16[1024,128]{1,0:T(8,128)(2,1)}, u32[]{:S(2)}, u32[]{:S(2)}) %collective-permute-start) | collective-permute-done | bytes 262176 | tf_op jit(solution)/shard_map/while/body/eval_jaxpr/ppermute | solution.py:28
  122.3 6.0 %collective-permute-done = bf16[1024,128]{1,0:T(8,128)(2,1)} collective-permute-done((bf16[1024,128]{1,0:T(8,128)(2,1)S(1)}, bf16[1024,128]{1,0:T(8,128)(2,1)}, u32[]{:S(2)}, u32[]{:S(2)}) %collective-permute-start) | collective-permute-done | bytes 262176 | tf_op jit(solution)/shard_map/while/body/eval_jaxpr/ppermute | solution.py:28
  133.1 7.1 %collective-permute-done = bf16[1024,128]{1,0:T(8,128)(2,1)} collective-permute-done((bf16[1024,128]{1,0:T(8,128)(2,1)S(1)}, bf16[1024,128]{1,0:T(8,128)(2,1)}, u32[]{:S(2)}, u32[]{:S(2)}) %collective-permute-start) | collective-permute-done | bytes 262176 | tf_op jit(solution)/shard_map/while/body/eval_jaxpr/ppermute | solution.py:28
  144.9 8.3 %collective-permute-done = bf16[1024,128]{1,0:T(8,128)(2,1)} collective-permute-done((bf16[1024,128]{1,0:T(8,128)(2,1)S(1)}, bf16[1024,128]{1,0:T(8,128)(2,1)}, u32[]{:S(2)}, u32[]{:S(2)}) %collective-permute-start) | collective-permute-done | bytes 262176 | tf_op jit(solution)/shard_map/while/body/eval_jaxpr/ppermute | solution.py:28
  158.0 7.7 %collective-permute-done = bf16[1024,128]{1,0:T(8,128)(2,1)} collective-permute-done((bf16[1024,128]{1,0:T(8,128)(2,1)S(1)}, bf16[1024,128]{1,0:T(8,128)(2,1)}, u32[]{:S(2)}, u32[]{:S(2)}) %collective-permute-start) | collective-permute-done | bytes 262176 | tf_op jit(solution)/shard_map/while/body/eval_jaxpr/ppermute | solution.py:28
  170.5 6.9 %collective-permute-done = bf16[1024,128]{1,0:T(8,128)(2,1)} collective-permute-done((bf16[1024,128]{1,0:T(8,128)(2,1)S(1)}, bf16[1024,128]{1,0:T(8,128)(2,1)}, u32[]{:S(2)}, u32[]{:S(2)}) %collective-permute-start) | collective-permute-done | bytes 262176 | tf_op jit(solution)/shard_map/while/body/eval_jaxpr/ppermute | solution.py:28
  182.1 6.0 %collective-permute-done = bf16[1024,128]{1,0:T(8,128)(2,1)} collective-permute-done((bf16[1024,128]{1,0:T(8,128)(2,1)S(1)}, bf16[1024,128]{1,0:T(8,128)(2,1)}, u32[]{:S(2)}, u32[]{:S(2)}) %collective-permute-start) | collective-permute-done | bytes 262176 | tf_op jit(solution)/shard_map/while/body/eval_jaxpr/ppermute | solution.py:28
  192.8 5.7 %collective-permute-done = bf16[1024,128]{1,0:T(8,128)(2,1)} collective-permute-done((bf16[1024,128]{1,0:T(8,128)(2,1)S(1)}, bf16[1024,128]{1,0:T(8,128)(2,1)}, u32[]{:S(2)}, u32[]{:S(2)}) %collective-permute-start) | collective-permute-done | bytes 262176 | tf_op jit(solution)/shard_map/while/body/eval_jaxpr/ppermute | solution.py:28
  203.4 5.7 %collective-permute-done = bf16[1024,128]{1,0:T(8,128)(2,1)} collective-permute-done((bf16[1024,128]{1,0:T(8,128)(2,1)S(1)}, bf16[1024,128]{1,0:T(8,128)(2,1)}, u32[]{:S(2)}, u32[]{:S(2)}) %collective-permute-start) | collective-permute-done | bytes 262176 | tf_op jit(solution)/shard_map/while/body/eval_jaxpr/ppermute | solution.py:28
  213.9 5.7 %collective-permute-done = bf16[1024,128]{1,0:T(8,128)(2,1)} collective-permute-done((bf16[1024,128]{1,0:T(8,128)(2,1)S(1)}, bf16[1024,128]{1,0:T(8,128)(2,1)}, u32[]{:S(2)}, u32[]{:S(2)}) %collective-permute-start) | collective-permute-done | bytes 262176 | tf_op jit(solution)/shard_map/while/body/eval_jaxpr/ppermute | solution.py:28
  219.6 2.4 copy.13
  222.0 2.6 convolution_add_fusion
  224.6 2.4 copy.14
  227.0 2.6 copy.20
  231.5 114.4 %all-reduce.1 = bf16[8,128,6,128]{1,0,3,2:T(8,128)(2,1)S(1)} all-reduce(f32[8,128,6,128]{1,0,3,2:T(8,128)} %broadcast_multiply_fusion), channel_id=1, replica_groups=mesh['row'=16,'col'=4,'depth'=8] {'depth'}, use_global_device_ids=true, to_apply=%region_2.3 | all-reduce | flops 786432 | bytes 4718592 | tf_op jit(solution)/shard_map/psum | solution.py:70
  (69 shorter events, 77.9 us)
Async XLA Ops:
  0.0 14.7 %copy-start = (s32[1,8]{1,0:T(1,128)S(1)}, s32[1,8]{1,0:T(1,128)}, u32[]{:S(2)}) copy-start(s32[1,8]{1,0:T(1,128)} %param.13) | copy-start | bytes 100
  4.0 10.6 %copy-start.2 = (s32[8,6]{1,0:T(8,128)S(1)}, s32[8,6]{1,0:T(8,128)}, u32[]{:S(2)}) copy-start(s32[8,6]{1,0:T(8,128)} %param.12) | copy-start | bytes 580
  4.0 13.3 %copy-start.3 = (s32[8,1]{0,1:T(1,128)S(1)}, s32[8,1]{0,1:T(1,128)}, u32[]{:S(2)}) copy-start(s32[8,1]{0,1:T(1,128)} %param.10) | copy-start | bytes 100
  4.0 13.4 %copy-start.1 = (bf16[1024,128]{1,0:T(8,128)(2,1)S(1)}, bf16[1024,128]{1,0:T(8,128)(2,1)}, u32[]{:S(2)}) copy-start(bf16[1024,128]{1,0:T(8,128)(2,1)} %param.8) | copy-start | bytes 786436
  4.0 46.0 %all-to-all-start = ((bf16[4,4,1,128,768]{4,3,1,2,0:T(8,128)(2,1)}), bf16[4,4,1,128,768]{4,3,1,2,0:T(8,128)(2,1)}, u32[]{:S(2)}, u32[]{:S(2)}) async-start(bf16[4,4,1,128,768]{4,3,1,2,0:T(8,128)(2,1)} %stack.3), calls=%async_computation | async-start | bytes 6291456 | tf_op jit(solution)/shard_map/all_to_all | solution.py:12
  50.9 12.5 %collective-permute-start = (bf16[1024,128]{1,0:T(8,128)(2,1)S(1)}, bf16[1024,128]{1,0:T(8,128)(2,1)}, u32[]{:S(2)}, u32[]{:S(2)}) collective-permute-start(bf16[1024,128]{1,0:T(8,128)(2,1)S(1)} %copy.30), channel_id=1, source_target_pairs={{480,0},{0,32},{32,64},{64,96},{96,128},{128,160},{160,192},{192,2... | collective-permute-start | bytes 786440 | tf_op jit(solution)/shard_map/while/body/eval_jaxpr/ppermute | solution.py:28
  64.4 10.8 %collective-permute-start = (bf16[1024,128]{1,0:T(8,128)(2,1)S(1)}, bf16[1024,128]{1,0:T(8,128)(2,1)}, u32[]{:S(2)}, u32[]{:S(2)}) collective-permute-start(bf16[1024,128]{1,0:T(8,128)(2,1)S(1)} %copy.30), channel_id=1, source_target_pairs={{480,0},{0,32},{32,64},{64,96},{96,128},{128,160},{160,192},{192,2... | collective-permute-start | bytes 786440 | tf_op jit(solution)/shard_map/while/body/eval_jaxpr/ppermute | solution.py:28
  76.1 9.8 %collective-permute-start = (bf16[1024,128]{1,0:T(8,128)(2,1)S(1)}, bf16[1024,128]{1,0:T(8,128)(2,1)}, u32[]{:S(2)}, u32[]{:S(2)}) collective-permute-start(bf16[1024,128]{1,0:T(8,128)(2,1)S(1)} %copy.30), channel_id=1, source_target_pairs={{480,0},{0,32},{32,64},{64,96},{96,128},{128,160},{160,192},{192,2... | collective-permute-start | bytes 786440 | tf_op jit(solution)/shard_map/while/body/eval_jaxpr/ppermute | solution.py:28
  86.9 9.6 %collective-permute-start = (bf16[1024,128]{1,0:T(8,128)(2,1)S(1)}, bf16[1024,128]{1,0:T(8,128)(2,1)}, u32[]{:S(2)}, u32[]{:S(2)}) collective-permute-start(bf16[1024,128]{1,0:T(8,128)(2,1)S(1)} %copy.30), channel_id=1, source_target_pairs={{480,0},{0,32},{32,64},{64,96},{96,128},{128,160},{160,192},{192,2... | collective-permute-start | bytes 786440 | tf_op jit(solution)/shard_map/while/body/eval_jaxpr/ppermute | solution.py:28
  97.4 9.6 %collective-permute-start = (bf16[1024,128]{1,0:T(8,128)(2,1)S(1)}, bf16[1024,128]{1,0:T(8,128)(2,1)}, u32[]{:S(2)}, u32[]{:S(2)}) collective-permute-start(bf16[1024,128]{1,0:T(8,128)(2,1)S(1)} %copy.30), channel_id=1, source_target_pairs={{480,0},{0,32},{32,64},{64,96},{96,128},{128,160},{160,192},{192,2... | collective-permute-start | bytes 786440 | tf_op jit(solution)/shard_map/while/body/eval_jaxpr/ppermute | solution.py:28
  107.9 9.6 %collective-permute-start = (bf16[1024,128]{1,0:T(8,128)(2,1)S(1)}, bf16[1024,128]{1,0:T(8,128)(2,1)}, u32[]{:S(2)}, u32[]{:S(2)}) collective-permute-start(bf16[1024,128]{1,0:T(8,128)(2,1)S(1)} %copy.30), channel_id=1, source_target_pairs={{480,0},{0,32},{32,64},{64,96},{96,128},{128,160},{160,192},{192,2... | collective-permute-start | bytes 786440 | tf_op jit(solution)/shard_map/while/body/eval_jaxpr/ppermute | solution.py:28
  118.5 9.8 %collective-permute-start = (bf16[1024,128]{1,0:T(8,128)(2,1)S(1)}, bf16[1024,128]{1,0:T(8,128)(2,1)}, u32[]{:S(2)}, u32[]{:S(2)}) collective-permute-start(bf16[1024,128]{1,0:T(8,128)(2,1)S(1)} %copy.30), channel_id=1, source_target_pairs={{480,0},{0,32},{32,64},{64,96},{96,128},{128,160},{160,192},{192,2... | collective-permute-start | bytes 786440 | tf_op jit(solution)/shard_map/while/body/eval_jaxpr/ppermute | solution.py:28
  129.2 10.9 %collective-permute-start = (bf16[1024,128]{1,0:T(8,128)(2,1)S(1)}, bf16[1024,128]{1,0:T(8,128)(2,1)}, u32[]{:S(2)}, u32[]{:S(2)}) collective-permute-start(bf16[1024,128]{1,0:T(8,128)(2,1)S(1)} %copy.30), channel_id=1, source_target_pairs={{480,0},{0,32},{32,64},{64,96},{96,128},{128,160},{160,192},{192,2... | collective-permute-start | bytes 786440 | tf_op jit(solution)/shard_map/while/body/eval_jaxpr/ppermute | solution.py:28
  141.1 12.1 %collective-permute-start = (bf16[1024,128]{1,0:T(8,128)(2,1)S(1)}, bf16[1024,128]{1,0:T(8,128)(2,1)}, u32[]{:S(2)}, u32[]{:S(2)}) collective-permute-start(bf16[1024,128]{1,0:T(8,128)(2,1)S(1)} %copy.30), channel_id=1, source_target_pairs={{480,0},{0,32},{32,64},{64,96},{96,128},{128,160},{160,192},{192,2... | collective-permute-start | bytes 786440 | tf_op jit(solution)/shard_map/while/body/eval_jaxpr/ppermute | solution.py:28
  154.2 11.5 %collective-permute-start = (bf16[1024,128]{1,0:T(8,128)(2,1)S(1)}, bf16[1024,128]{1,0:T(8,128)(2,1)}, u32[]{:S(2)}, u32[]{:S(2)}) collective-permute-start(bf16[1024,128]{1,0:T(8,128)(2,1)S(1)} %copy.30), channel_id=1, source_target_pairs={{480,0},{0,32},{32,64},{64,96},{96,128},{128,160},{160,192},{192,2... | collective-permute-start | bytes 786440 | tf_op jit(solution)/shard_map/while/body/eval_jaxpr/ppermute | solution.py:28
  166.6 10.7 %collective-permute-start = (bf16[1024,128]{1,0:T(8,128)(2,1)S(1)}, bf16[1024,128]{1,0:T(8,128)(2,1)}, u32[]{:S(2)}, u32[]{:S(2)}) collective-permute-start(bf16[1024,128]{1,0:T(8,128)(2,1)S(1)} %copy.30), channel_id=1, source_target_pairs={{480,0},{0,32},{32,64},{64,96},{96,128},{128,160},{160,192},{192,2... | collective-permute-start | bytes 786440 | tf_op jit(solution)/shard_map/while/body/eval_jaxpr/ppermute | solution.py:28
  178.3 9.8 %collective-permute-start = (bf16[1024,128]{1,0:T(8,128)(2,1)S(1)}, bf16[1024,128]{1,0:T(8,128)(2,1)}, u32[]{:S(2)}, u32[]{:S(2)}) collective-permute-start(bf16[1024,128]{1,0:T(8,128)(2,1)S(1)} %copy.30), channel_id=1, source_target_pairs={{480,0},{0,32},{32,64},{64,96},{96,128},{128,160},{160,192},{192,2... | collective-permute-start | bytes 786440 | tf_op jit(solution)/shard_map/while/body/eval_jaxpr/ppermute | solution.py:28
  189.0 9.6 %collective-permute-start = (bf16[1024,128]{1,0:T(8,128)(2,1)S(1)}, bf16[1024,128]{1,0:T(8,128)(2,1)}, u32[]{:S(2)}, u32[]{:S(2)}) collective-permute-start(bf16[1024,128]{1,0:T(8,128)(2,1)S(1)} %copy.30), channel_id=1, source_target_pairs={{480,0},{0,32},{32,64},{64,96},{96,128},{128,160},{160,192},{192,2... | collective-permute-start | bytes 786440 | tf_op jit(solution)/shard_map/while/body/eval_jaxpr/ppermute | solution.py:28
  199.5 9.6 %collective-permute-start = (bf16[1024,128]{1,0:T(8,128)(2,1)S(1)}, bf16[1024,128]{1,0:T(8,128)(2,1)}, u32[]{:S(2)}, u32[]{:S(2)}) collective-permute-start(bf16[1024,128]{1,0:T(8,128)(2,1)S(1)} %copy.30), channel_id=1, source_target_pairs={{480,0},{0,32},{32,64},{64,96},{96,128},{128,160},{160,192},{192,2... | collective-permute-start | bytes 786440 | tf_op jit(solution)/shard_map/while/body/eval_jaxpr/ppermute | solution.py:28
  210.1 9.6 %collective-permute-start = (bf16[1024,128]{1,0:T(8,128)(2,1)S(1)}, bf16[1024,128]{1,0:T(8,128)(2,1)}, u32[]{:S(2)}, u32[]{:S(2)}) collective-permute-start(bf16[1024,128]{1,0:T(8,128)(2,1)S(1)} %copy.30), channel_id=1, source_target_pairs={{480,0},{0,32},{32,64},{64,96},{96,128},{128,160},{160,192},{192,2... | collective-permute-start | bytes 786440 | tf_op jit(solution)/shard_map/while/body/eval_jaxpr/ppermute | solution.py:28
